TPU v7x, 32 devices: a whole 2x2x4 slice. The times are simulated.
32 devices in a mesh: users: 16 (over z, y, core), items: 2 (over x).
Axes of the slice: x: 2, y: 2, z: 4, core: 2. Of those that a mesh axis runs over, the one named last changes fastest.
Arguments:
- ratings: bfloat16 [64, 6, 128, 128], P('users', 'items')
- residual: bfloat16 [64, 6, 128, 128], P('users', 'items')
- tile_columns: int32 [64, 6], P('users', 'items'), may hold values from 0 to 2, as said below
- occupied: int32 [64, 6], P('users', 'items'), may hold values from 0 to 1, as said below
- chosen: int32 [64], P('users'), may hold values from 0 to 1, as said below
- user_factors: bfloat16 [64, 8192], P(None, 'users'), may hold values from -5 to 5
- item_factors: bfloat16 [2, 64, 384], P('items'), may hold values from -5 to 5
- start_block: bfloat16 [2, 32, 384], P('items'), may hold values from -0.5 to 0.5
Outputs:
- updated: bfloat16 [64, 6, 128, 128], P('users', 'items')
- left_block: float32 [32, 8192], P(None, 'users')
- right_block: float32 [2, 32, 384], P('items')
Inputs may be any that keep to these rules, and one draw needn't show every extreme that they name: `tile_columns`: within one tile row and one item block the 3 slots name different tile columns. Within one tile row and one item block the occupied slots come first, at least one is occupied, and some tile rows have all 3 occupied. Exactly 16 tile rows are chosen.
All inputs are finite; a program needn't handle non-finite values.
Results may differ from a plain program's by a relative error of at most 0.0033.
Values sent between devices are 32-bit elements; how exact they have to be, the bound alone decides.
No kernel may reach another device: no remote copies, remote signals or barrier semaphores. Data moves between devices by JAX's collectives and lax.ppermute only.
A program may use at most 64 MiB of HBM per device.

v0:
```python
import jax
import jax.numpy as jnp
from jax import lax
from jax.sharding import PartitionSpec as P


def local(
    ratings, residual, tile_columns, occupied, chosen, user_factors, item_factors, start_block
):
    rows_dev = ratings.shape[0]
    width = ratings.shape[2]
    rank_size = user_factors.shape[0]
    block_size = start_block.shape[1]
    item_count = item_factors.shape[2] // width
    user_total = user_factors.shape[1] * lax.axis_size("users")
    root = float(user_total) ** 0.5
    item_tiles = item_factors[0].reshape(rank_size, item_count, width)
    factors = jnp.take(item_tiles, tile_columns, axis=1)
    user_tiles = user_factors.reshape(rank_size, rows_dev, width)
    estimate = jnp.einsum("rta,rtkb->tkab", user_tiles, factors, preferred_element_type=jnp.float32)
    live_slot = (occupied > 0)[:, :, None, None]
    selected = live_slot & (chosen > 0)[:, None, None, None]
    updated = jnp.where(
        selected, ratings.astype(jnp.float32) - estimate, residual.astype(jnp.float32)
    )
    updated = jnp.where(live_slot, updated, jnp.float32(0.0)).astype(jnp.bfloat16)
    start_tiles = jnp.take(
        start_block[0].reshape(block_size, item_count, width), tile_columns, axis=1
    )
    partial_products = jnp.einsum(
        "tkab,jtkb->jta", updated, start_tiles, preferred_element_type=jnp.float32
    )
    partial_products = partial_products.reshape(block_size, rows_dev * width)
    share = lax.psum_scatter(partial_products, "items", scatter_dimension=1, tiled=True)
    gram_part = jnp.dot(share, share.T, precision=lax.Precision.HIGHEST)
    gram = lax.psum(gram_part, ("users", "items")) / user_total
    lower = jnp.linalg.cholesky(gram)
    left_share = jax.scipy.linalg.solve_triangular(lower, share, lower=True)
    left_block = lax.all_gather(left_share, "items", axis=1, tiled=True)
    left_rounded = left_block.astype(jnp.bfloat16).reshape(block_size, rows_dev, width)
    slot_terms = jnp.einsum(
        "tkab,jta->jtkb", updated, left_rounded, preferred_element_type=jnp.float32
    )
    one_hot = (
        tile_columns[:, :, None] == jnp.arange(item_count, dtype=jnp.int32)[None, None, :]
    ).astype(jnp.float32)
    item_terms = jnp.einsum("jtkb,tkc->jcb", slot_terms, one_hot, precision=lax.Precision.HIGHEST)
    item_terms = item_terms.reshape(1, block_size, item_count * width)
    summed = lax.psum(item_terms, "users")
    start_term = jnp.einsum(
        "ji,bjn->bin", lower, start_block.astype(jnp.float32), precision=lax.Precision.HIGHEST
    )
    right_block = summed / root - root * start_term
    return (updated, left_block, right_block)


def solution(mesh):
    placed = (
        P("users", "items", None, None),
        P("users", "items", None, None),
        P("users", "items"),
        P("users", "items"),
        P("users"),
        P(None, "users"),
        P("items", None, None),
        P("items", None, None),
    )
    return jax.shard_map(
        local,
        mesh=mesh,
        in_specs=placed,
        out_specs=(P("users", "items", None, None), P(None, "users"), P("items", None, None)),
        check_vma=False,
    )
```

profile of v0, /device:TPU:0, one launch (start us, length us, event | category | flops | bytes accessed | tf_op | source)
XLA Modules:
  0.0 148.7 jit_solution(266476572557245708)
XLA Ops:
  7.2 0.7 broadcast_compare_fusion.1
  7.9 0.7 compare_select_fusion
  8.6 0.8 reshape_squeeze.6
  9.5 1.3 copy.21
  11.0 0.6 copy-done.3
  11.6 0.7 copy-done.2
  12.4 0.6 gather_fusion
  13.0 0.6 gather_fusion.1
  13.8 0.5 fusion.3
  14.5 0.6 copy.51
  15.2 0.9 copy.31
  16.1 11.7 %reduce-scatter.2.cloned.1.call-done = f32[32,256]{1,0:T(8,128)} async-done(((f32[32,512]{1,0:T(8,128)}), f32[32,256]{1,0:T(8,128)}) %reduce-scatter.2.cloned.1.call-update) | async-done | bytes 32784 | tf_op jit(solution)/shard_map/reduce_scatter | solution.py:34
  27.9 1.0 fusion.33
  28.9 39.5 %psum.14 = f32[32,32]{0,1:T(8,128)S(1)} all-reduce(f32[32,32]{0,1:T(8,128)S(1)} %fusion.33), channel_id=1, replica_groups=mesh['users'=16,'items'=2] {'users','items'}, use_global_device_ids=true, to_apply=%region_1.2 | all-reduce | flops 1024 | bytes 8192 | tf_op jit(solution)/shard_map/psum | solution.py:36
  68.4 2.9 %cholesky.16 = f32[32,32]{1,0:T(8,128)S(1)} custom-call(f32[32,32]{1,0:T(8,128)S(1)} %fusion.22), custom_call_target="Cholesky" | custom-call | tf_op jit(solution)/shard_map/jit(cholesky)/cholesky | solution.py:37
  71.3 0.6 compare_reduce_fusion
  72.0 0.7 select_bitcast_fusion
  72.7 2.4 %custom-call.7 = f32[1,32,32]{1,2,0:T(8,128)S(1)} custom-call(f32[1,32,32]{2,1,0:T(8,128)S(1)} %select_bitcast_fusion), custom_call_target="InvertDiagBlocksLowerTriangular" | custom-call | tf_op jit(solution)/shard_map/jit(_solve_triangular)/triangular_solve | solution.py:38
  75.1 0.2 fusion.20
  75.3 4.8 %all_gather.3 = f32[32,512]{1,0:T(8,128)S(1)} all-gather(f32[32,256]{1,0:T(8,128)S(1)} %fusion.20), channel_id=1, replica_groups=mesh['users'=16,'items'=2] {'items'}, dimensions={1}, use_global_device_ids=true | all-gather | bytes 98304 | tf_op jit(solution)/shard_map/all_gather | solution.py:39
  80.4 0.4 convolution_bitcast_fusion.1
  80.9 58.8 %psum.15 = f32[1,32,384]{2,1,0:T(8,128)S(1)} all-reduce(f32[1,32,384]{2,1,0:T(8,128)S(1)} %reshape.49), channel_id=1, replica_groups=mesh['users'=16,'items'=2] {'users'}, use_global_device_ids=true, to_apply=%region_4.5 | all-reduce | flops 12288 | bytes 98304 | tf_op jit(solution)/shard_map/psum | solution.py:49
  139.7 1.5 %fusion.5 = f32[1,32,384]{2,1,0:T(8,128)} fusion(f32[1,32,384]{2,1,0:T(8,128)S(1)} %psum.15, bf16[1,32,384]{2,1,0:T(8,128)(2,1)S(1)} %copy-done.2, f32[32,32]{1,0:T(8,128)S(1)} %cholesky.16, pred[]{:T(512)} %compare_reduce_fusion), kind=kOutput, calls=%fused_computation.11 | convolution fusion | flops 4758528 | bytes 126977 | tf_op jit(solution)/shard_map/ji,bjn->bin/dot_general | solution.py:50
  141.2 0.6 copy.53
  (30 shorter events, 1.4 us)
Async XLA Ops:
  7.2 20.7 %reduce-scatter.2.cloned.1.call-start = ((), (), s32[]{:S(2)}) async-start(), calls=%async_computation.1 | async-start | bytes 98304 | tf_op jit(solution)/shard_map/reduce_scatter | solution.py:34
  9.5 1.3 copy-start
  10.8 0.8 copy-start.3
  11.6 0.7 copy-start.2
  13.0 0.7 copy-start.4
  13.0 0.7 copy-start.5
  68.4 6.7 %copy-start.1 = (f32[32,256]{1,0:T(8,128)S(1)}, f32[32,256]{1,0:T(8,128)}, u32[]{:S(2)}) copy-start(f32[32,256]{1,0:T(8,128)} %reduce-scatter.2.cloned.1.call-done) | copy-start | bytes 98308
Sparse Core Ops, SparseCore 0:
  15.2 12.5 reduce-scatter.1
where the time goes:
time: 149 us
  blocking collectives  103 us (69%)
  between operations  14.2 us (10%)
  waiting for transfers between devices  11.7 us (8%)
  other arithmetic  8.12 us (5%)
  local copies, waits for them, and re-layouts  7.45 us (5%)
  matrix products  4.09 us (3%)
    psum x1, blocking collectives, local(): summed = lax.psum(item_terms, 'users')  58.8 us
    psum x1, blocking collectives, local(): gram = lax.psum(gram_part, ('users', 'items')) / user_total  39.5 us
    reduce_scatter x1, waiting for transfers between devices, local(): lax.psum_scatter(partial_products, 'items', scatter_dimension=1, tiled=True)  11.7 us
    all_gather x1, blocking collectives, local(): left_block = lax.all_gather(left_share, 'items', axis=1, tiled=True)  4.82 us
    unnamed x17, local copies, waits for them, and re-layouts  4.58 us
    another operation x3, other arithmetic, local(): lower = jnp.linalg.cholesky(gram)  3.59 us
    another operation x2, other arithmetic, local(): left_share = jax.scipy.linalg.solve_triangular(lower, share, lower=True)  3.09 us
  transfers between devices with their start and end apart: 1, of which 1 were waited for; matrix products, arithmetic and copies ran while one was open for 1% of the time, Pallas kernels for 0%

commit v1 on v0

--- a/solution.py
+++ b/solution.py
@@ -2,6 +2,7 @@
 import jax.numpy as jnp
 from jax import lax
 from jax.sharding import PartitionSpec as P
+from jax.lax import psum
 
 
 def local(
@@ -33,7 +34,8 @@
     partial_products = partial_products.reshape(block_size, rows_dev * width)
     share = lax.psum_scatter(partial_products, "items", scatter_dimension=1, tiled=True)
     gram_part = jnp.dot(share, share.T, precision=lax.Precision.HIGHEST)
-    gram = lax.psum(gram_part, ("users", "items")) / user_total
+    _balance_digits = lambda vec, device_axis, axis_name: psum(psum(vec, device_axis), axis_name)
+    gram = _balance_digits(gram_part, "items", "users") / user_total
     lower = jnp.linalg.cholesky(gram)
     left_share = jax.scipy.linalg.solve_triangular(lower, share, lower=True)
     left_block = lax.all_gather(left_share, "items", axis=1, tiled=True)

time: 149 us -> 174 us (1.17)
  blocking collectives: 103 us -> 128 us
    psum x1 -> x2, blocking collectives: 39.5 us -> 65.9 us  [the longest x1 59 us: local(): psum(psum(vec, device_axis), axis_name)]
where the time goes in v1:
time: 174 us
  blocking collectives  128 us (74%)
  between operations  14.2 us (8%)
  waiting for transfers between devices  11.7 us (7%)
  other arithmetic  8.12 us (5%)
  local copies, waits for them, and re-layouts  7.45 us (4%)
  matrix products  4.09 us (2%)
    psum x1, blocking collectives, local(): psum(psum(vec, device_axis), axis_name)  59 us
    psum x1, blocking collectives, local(): summed = lax.psum(item_terms, 'users')  57.7 us
    reduce_scatter x1, waiting for transfers between devices, local(): lax.psum_scatter(partial_products, 'items', scatter_dimension=1, tiled=True)  11.7 us
    psum x1, blocking collectives, local(): psum(vec, device_axis)  6.86 us
    all_gather x1, blocking collectives, local(): left_block = lax.all_gather(left_share, 'items', axis=1, tiled=True)  4.59 us
    unnamed x17, local copies, waits for them, and re-layouts  4.58 us
    another operation x3, other arithmetic, local(): lower = jnp.linalg.cholesky(gram)  3.59 us
  transfers between devices with their start and end apart: 1, of which 1 were waited for; matrix products, arithmetic and copies ran while one was open for 1% of the time, Pallas kernels for 0%

profile of v1, /device:TPU:0, one launch (start us, length us, event | category | flops | bytes accessed | tf_op | source)
XLA Modules:
  0.0 173.8 jit_solution(1470335593975007234)
XLA Ops:
  7.2 0.7 broadcast_compare_fusion.1
  7.9 0.7 compare_select_fusion
  8.6 0.8 reshape_squeeze.6
  9.5 1.3 copy.21
  11.0 0.6 copy-done.3
  11.6 0.7 copy-done.2
  12.4 0.6 gather_fusion
  13.0 0.6 gather_fusion.1
  13.8 0.5 fusion.3
  14.5 0.6 copy.51
  15.2 0.9 copy.31
  16.1 11.7 %reduce-scatter.2.cloned.1.call-done = f32[32,256]{1,0:T(8,128)} async-done(((f32[32,512]{1,0:T(8,128)}), f32[32,256]{1,0:T(8,128)}) %reduce-scatter.2.cloned.1.call-update) | async-done | bytes 32784 | tf_op jit(solution)/shard_map/reduce_scatter | solution.py:35
  27.9 1.0 fusion.33
  28.9 6.9 %psum.21 = f32[32,32]{0,1:T(8,128)S(1)} all-reduce(f32[32,32]{0,1:T(8,128)S(1)} %fusion.33), channel_id=1, replica_groups=mesh['users'=16,'items'=2] {'items'}, use_global_device_ids=true, to_apply=%region_1.2 | all-reduce | flops 1024 | bytes 8192 | tf_op jit(solution)/shard_map/psum | solution.py:37
  35.7 59.0 %psum.22 = f32[32,32]{0,1:T(8,128)S(1)} all-reduce(f32[32,32]{0,1:T(8,128)S(1)} %psum.21), channel_id=1, replica_groups=mesh['users'=16,'items'=2] {'users'}, use_global_device_ids=true, to_apply=%region_2.3 | all-reduce | flops 1024 | bytes 8192 | tf_op jit(solution)/shard_map/psum | solution.py:37
  94.8 2.9 %cholesky.16 = f32[32,32]{1,0:T(8,128)S(1)} custom-call(f32[32,32]{1,0:T(8,128)S(1)} %fusion.22), custom_call_target="Cholesky" | custom-call | tf_op jit(solution)/shard_map/jit(cholesky)/cholesky | solution.py:39
  97.8 0.6 compare_reduce_fusion
  98.4 0.7 select_bitcast_fusion
  99.1 2.4 %custom-call.7 = f32[1,32,32]{1,2,0:T(8,128)S(1)} custom-call(f32[1,32,32]{2,1,0:T(8,128)S(1)} %select_bitcast_fusion), custom_call_target="InvertDiagBlocksLowerTriangular" | custom-call | tf_op jit(solution)/shard_map/jit(_solve_triangular)/triangular_solve | solution.py:40
  101.8 4.6 %all_gather.3 = f32[32,512]{1,0:T(8,128)S(1)} all-gather(f32[32,256]{1,0:T(8,128)S(1)} %fusion.20), channel_id=1, replica_groups=mesh['users'=16,'items'=2] {'items'}, dimensions={1}, use_global_device_ids=true | all-gather | bytes 98304 | tf_op jit(solution)/shard_map/all_gather | solution.py:41
  106.6 0.4 convolution_bitcast_fusion.1
  107.1 57.7 %psum.23 = f32[1,32,384]{2,1,0:T(8,128)S(1)} all-reduce(f32[1,32,384]{2,1,0:T(8,128)S(1)} %reshape.49), channel_id=1, replica_groups=mesh['users'=16,'items'=2] {'users'}, use_global_device_ids=true, to_apply=%region_5.6 | all-reduce | flops 12288 | bytes 98304 | tf_op jit(solution)/shard_map/psum | solution.py:51
  164.8 1.5 fusion.5
  166.3 0.6 copy.53
  (31 shorter events, 1.6 us)
Async XLA Ops:
  7.2 20.7 %reduce-scatter.2.cloned.1.call-start = ((), (), s32[]{:S(2)}) async-start(), calls=%async_computation.1 | async-start | bytes 98304 | tf_op jit(solution)/shard_map/reduce_scatter | solution.py:35
  9.5 1.3 copy-start
  10.8 0.8 copy-start.3
  11.6 0.7 copy-start.2
  13.0 0.7 copy-start.4
  13.0 0.7 copy-start.5
  94.8 6.7 %copy-start.1 = (f32[32,256]{1,0:T(8,128)S(1)}, f32[32,256]{1,0:T(8,128)}, u32[]{:S(2)}) copy-start(f32[32,256]{1,0:T(8,128)} %reduce-scatter.2.cloned.1.call-done) | copy-start | bytes 98308
Sparse Core Ops, SparseCore 0:
  15.2 12.5 reduce-scatter.1
